TPU v7x, 128 devices: a whole 4x4x4 slice. The times are simulated.
128 devices in a mesh: req: 2 (over core), seq: 64 (over z, y, x).
Axes of the slice: x: 4, y: 4, z: 4, core: 2. Of those that a mesh axis runs over, the one named last changes fastest.
Arguments:
- tokens: bfloat16 [4, 128, 1536], P(None, ('req', 'seq')), may hold values from -6 to 6
- lengths: int32 [128], P('req'), may hold values from 1 to 16384, as said below
- k_cache: bfloat16 [128, 4096, 256], P('req', 'seq'), may hold values from -500 to 500
- v_cache: bfloat16 [128, 4096, 256], P('req', 'seq'), may hold values from -12 to 12
- attn_gain: bfloat16 [1536], replicated, may hold values from 0.5 to 1.5
- w_qkv: bfloat16 [1536, 2048], replicated, may hold values from -0.15625 to 0.15625
- sink: float32 [12], replicated, may hold values from -1 to 3
- w_out: bfloat16 [1536, 1536], replicated, may hold values from -0.15625 to 0.15625
- moe_gain: bfloat16 [1536], replicated, may hold values from 0.5 to 1.5
- router: bfloat16 [1536, 32], replicated, may hold values from -0.15625 to 0.15625
- w_gate: bfloat16 [1536, 24576], P(None, ('req', 'seq')), may hold values from -0.15625 to 0.15625
- w_up: bfloat16 [1536, 24576], P(None, ('req', 'seq')), may hold values from -0.15625 to 0.15625
- w_down: bfloat16 [24576, 1536], P(('req', 'seq')), may hold values from -0.21875 to 0.21875
- routes: int32 [128, 4, 4], replicated, may hold values from 0 to 31, all different within a row; in each aligned block of 4 rows (0 to 3, 4 to 7, ..., all dimensions but the last counted through in order) at most 2 rows name the same one
Outputs:
- outputs: bfloat16 [4, 128, 1536], P(None, ('req', 'seq'))
Inputs may be any that keep to these rules, and one draw needn't show every extreme that they name: Each request has lengths positions before the first step; some request has all 16384 in every draw. `routes`: among the 4 tokens of one device's requests (requests 1 d .. 1 d + 1 - 1, all steps), no expert is named by more than 2 tokens, and in every draw some expert is named by exactly 2.
All inputs are finite; a program needn't handle non-finite values.
Results may differ from a plain program's by a relative error of at most 0.02.
Values may be sent and summed in bfloat16 or wider, within the bound.
No kernel may reach another device: no remote copies, remote signals or barrier semaphores. Data moves between devices by JAX's collectives and lax.ppermute only.
A program may use at most 512 MiB of HBM per device.

v0:
```python
import jax
import jax.numpy as jnp
from jax import lax
from jax.sharding import PartitionSpec as P

D = 1536
QH = 12
KVH = 2
HD = 128
E = 32
EFF = 768
TOP = 4
STEPS = 4
MOST = 2


def combined_all(value, axis, join):
    gathered = jax.tree.map(
        lambda a, kind: lax.all_gather(a.astype(kind), axis),
        value,
        (jnp.bfloat16, jnp.bfloat16, jnp.bfloat16),
    )

    def take(source):
        return jax.tree.map(
            lambda a, own: lax.dynamic_index_in_dim(a, source, 0, False).astype(own.dtype),
            gathered,
            value,
        )

    return lax.fori_loop(
        1, lax.axis_size(axis), lambda source, state: join(state, take(source)), take(0)
    )


def normalize(x, gain):
    xf = x.astype(jnp.float32)
    inv = lax.rsqrt(jnp.mean(xf * xf, axis=-1, keepdims=True) + 1e-05)
    return (xf * inv * gain.astype(jnp.float32)).astype(jnp.bfloat16)


def rotate(x, place):
    half = x.shape[-1] // 2
    index = jnp.arange(half, dtype=jnp.float32)
    inverse = jnp.exp(-jnp.log(1000000.0) * 2.0 * index / x.shape[-1])
    angle = place.astype(jnp.float32)[..., None, None] * inverse
    first = x[..., :half]
    second = x[..., half:]
    cosine = jnp.cos(angle)
    sine = jnp.sin(angle)
    return jnp.concatenate(
        [first * cosine - second * sine, second * cosine + first * sine], axis=-1
    )


def route_weights(logits, picks):
    onehot = (picks[:, :, None] == jnp.arange(E, dtype=jnp.int32)[None, None, :]).astype(
        jnp.float32
    )
    chosen = jnp.sum(onehot * logits[:, None, :], axis=-1)
    share = jax.nn.softmax(chosen, axis=-1)
    return jnp.sum(share[:, :, None] * onehot, axis=1)


def combine_parts(first, second):
    peak = jnp.maximum(first[0], second[0])
    left_scale = jnp.exp(first[0] - peak)
    right_scale = jnp.exp(second[0] - peak)
    return (
        peak,
        first[1] * left_scale + second[1] * right_scale,
        first[2] * left_scale[..., None] + second[2] * right_scale[..., None],
    )


def on_device(
    tokens,
    lengths,
    k_cache,
    v_cache,
    attn_gain,
    w_qkv,
    sink,
    w_out,
    moe_gain,
    router,
    w_gate,
    w_up,
    w_down,
    routes,
):
    seq_count = lax.axis_size("seq")
    seq_place = lax.axis_index("seq")
    device = lax.axis_index("req") * seq_count + seq_place
    devices = lax.axis_size(("req", "seq"))
    rows = tokens.shape[1]
    group_rows = lengths.shape[0]
    local_pos = k_cache.shape[1]
    window = local_pos * seq_count
    heads_per = QH // KVH
    scale = HD ** (-0.5)
    columns = w_gate.shape[1]
    expert_mine = device * columns // EFF
    own_len = lax.dynamic_slice_in_dim(lengths, seq_place * rows, rows)
    step_ids = jnp.arange(STEPS, dtype=jnp.int32)
    a = normalize(tokens, attn_gain)
    proj = jnp.einsum("srm,mn->srn", a, w_qkv, preferred_element_type=jnp.float32)
    place = own_len[None, :] + step_ids[:, None]
    query = rotate(proj[..., : QH * HD].reshape(STEPS, rows, QH, HD), place).astype(jnp.bfloat16)
    fresh_key = rotate(
        proj[..., QH * HD : (QH + KVH) * HD].reshape(STEPS, rows, KVH, HD), place
    ).astype(jnp.bfloat16)
    fresh_val = proj[..., (QH + KVH) * HD :].reshape(STEPS, rows, KVH, HD).astype(jnp.bfloat16)
    every_query = lax.all_gather(query.reshape(STEPS, rows, QH * HD), "seq", axis=1, tiled=True)
    grouped_all = every_query.reshape(STEPS, group_rows, KVH, heads_per, HD)
    cache_keys = k_cache.reshape(group_rows, local_pos, KVH, HD)
    cache_vals = v_cache.reshape(group_rows, local_pos, KVH, HD)
    scores = (
        jnp.einsum("tnkgd,nckd->tnkgc", grouped_all, cache_keys, preferred_element_type=jnp.float32)
        * scale
    )
    key_slot = seq_place * local_pos + jnp.arange(local_pos, dtype=jnp.int32)
    back = jnp.mod(lengths[None, :, None] - 1 - key_slot[None, None, :], window)
    reach = jnp.minimum(lengths[None, :, None], window - 1 - step_ids[:, None, None])
    valid = (back < reach)[:, :, None, None, :]
    peak_local = jnp.max(jnp.where(valid, scores, -1e30), axis=-1)
    weights = jnp.where(valid, jnp.exp(scores - peak_local[..., None]), 0.0)
    total_local = jnp.sum(weights, axis=-1)
    mixed_local = jnp.einsum(
        "tnkgc,nckd->tnkgd",
        weights.astype(jnp.bfloat16),
        cache_vals,
        preferred_element_type=jnp.float32,
    )
    peak_all, total_all, mixed_all = combined_all(
        (peak_local, total_local, mixed_local), "seq", combine_parts
    )
    peak = lax.dynamic_slice_in_dim(peak_all, seq_place * rows, rows, 1)
    total = lax.dynamic_slice_in_dim(total_all, seq_place * rows, rows, 1)
    mixed = lax.dynamic_slice_in_dim(mixed_all, seq_place * rows, rows, 1)
    grouped = query.reshape(STEPS, rows, KVH, heads_per, HD)
    tail_scores = (
        jnp.einsum("trkgd,srkd->trkgs", grouped, fresh_key, preferred_element_type=jnp.float32)
        * scale
    )
    tail_valid = (step_ids[None, :] <= step_ids[:, None])[:, None, None, None, :]
    sink_grid = sink.reshape(KVH, heads_per)[None, None]
    final = jnp.maximum(
        jnp.maximum(peak, jnp.max(jnp.where(tail_valid, tail_scores, -1e30), axis=-1)), sink_grid
    )
    shift = jnp.exp(peak - final)
    tail_w = jnp.where(tail_valid, jnp.exp(tail_scores - final[..., None]), 0.0)
    denom = total * shift + jnp.sum(tail_w, axis=-1) + jnp.exp(sink_grid - final)
    mixed = mixed * shift[..., None] + jnp.einsum(
        "trkgs,srkd->trkgd",
        tail_w.astype(jnp.bfloat16),
        fresh_val,
        preferred_element_type=jnp.float32,
    )
    attn = (mixed / denom[..., None]).reshape(STEPS, rows, QH * HD).astype(jnp.bfloat16)
    h = (
        tokens.astype(jnp.float32)
        + jnp.einsum("srn,nm->srm", attn, w_out, preferred_element_type=jnp.float32)
    ).astype(jnp.bfloat16)
    u = normalize(h, moe_gain)
    own_tokens = rows * STEPS
    u_tok = u.transpose(1, 0, 2).reshape(own_tokens, D)
    every_row = lax.all_gather(u_tok, ("req", "seq"), axis=0, tiled=True)
    all_picks = routes.reshape(-1, TOP)
    every_logit = jnp.dot(every_row, router, preferred_element_type=jnp.float32)
    dense_all = route_weights(every_logit, all_picks)
    weight_mine = jnp.sum(
        dense_all * (jnp.arange(E, dtype=jnp.int32) == expert_mine)[None, :].astype(jnp.float32),
        axis=-1,
    )
    mine = jnp.any(all_picks == expert_mine, axis=-1)
    slot = jnp.cumsum(mine.astype(jnp.int32)) - 1
    limit = MOST * devices
    select = (
        (slot[None, :] == jnp.arange(limit, dtype=jnp.int32)[:, None]) & mine[None, :]
    ).astype(jnp.float32)
    picked = jnp.dot(
        select.astype(jnp.bfloat16), every_row, preferred_element_type=jnp.float32
    ).astype(jnp.bfloat16)
    slot_weight = jnp.dot(select, weight_mine, precision=lax.Precision.HIGHEST)
    hidden = (
        jax.nn.relu(jnp.dot(picked, w_gate, preferred_element_type=jnp.float32))
        * jnp.dot(picked, w_up, preferred_element_type=jnp.float32)
    ).astype(jnp.bfloat16)
    produced = jnp.dot(hidden, w_down, preferred_element_type=jnp.float32) * slot_weight[:, None]
    moe = lax.psum_scatter(
        jnp.einsum("lc,lm->cm", select, produced, precision=lax.Precision.HIGHEST),
        ("req", "seq"),
        scatter_dimension=0,
        tiled=True,
    )
    moe_steps = moe.reshape(rows, STEPS, D).transpose(1, 0, 2)
    return (h.astype(jnp.float32) + moe_steps).astype(jnp.bfloat16)


def solution(mesh):
    in_specs = (
        P(None, ("req", "seq"), None),
        P("req"),
        P("req", "seq", None),
        P("req", "seq", None),
        P(),
        P(),
        P(),
        P(),
        P(),
        P(),
        P(None, ("req", "seq")),
        P(None, ("req", "seq")),
        P(("req", "seq"), None),
        P(),
    )
    out_specs = P(None, ("req", "seq"), None)
    return jax.shard_map(
        on_device, mesh=mesh, in_specs=in_specs, out_specs=out_specs, check_vma=False
    )
```

profile of v0, /device:TPU:1, one launch (start us, length us, event | category | flops | bytes accessed | tf_op | source)
XLA Modules:
  0.0 1043.7 jit_solution(8082044500679967716)
XLA Ops:
  8.2 3.9 convolution_bitcast_fusion.1
  17.0 155.1 %all_gather.20 = bf16[4,64,1536]{2,0,1:T(4,128)(2,1)S(1)} all-gather(bf16[4,1,1536]{2,0,1:T(4,128)(2,1)S(1)} %convert_element_type.198), channel_id=1, replica_groups=mesh['req'=2,'seq'=64] {'seq'}, dimensions={1}, use_global_device_ids=true | all-gather | bytes 798720 | tf_op jit(solution)/shard_map/all_gather | solution.py:114
  175.9 3.4 fusion.8
  184.5 149.0 %all-gather = bf16[256,64,2,6]{1,2,3,0:T(2,128)(2,1)S(1)} all-gather(bf16[4,64,2,6]{1,2,3,0:T(2,128)(2,1)S(1)} %copy.158), channel_id=2, replica_groups=mesh['req'=2,'seq'=64] {'seq'}, dimensions={0}, use_global_device_ids=true | all-gather | bytes 399360 | tf_op jit(solution)/shard_map/all_gather | solution.py:19
  333.5 156.4 %all-gather.1 = bf16[256,64,2,6]{1,2,3,0:T(2,128)(2,1)S(1)} all-gather(bf16[4,64,2,6]{1,2,3,0:T(2,128)(2,1)S(1)} %copy.160), channel_id=3, replica_groups=mesh['req'=2,'seq'=64] {'seq'}, dimensions={0}, use_global_device_ids=true | all-gather | bytes 399360 | tf_op jit(solution)/shard_map/all_gather | solution.py:19
  490.9 40.0 %all-gather.7.cloned.1.call-done = bf16[256,64,2,6,128]{4,3,0,2,1:T(8,128)(2,1)} async-done(((bf16[4,64,2,6,128]{4,3,0,2,1:T(8,128)(2,1)}), bf16[256,64,2,6,128]{4,3,0,2,1:T(8,128)(2,1)}) %all-gather.7.cloned.1.call-update) | async-done | bytes 50331664 | tf_op jit(solution)/shard_map/all_gather | solution.py:19
  532.5 233.8 %while.19 = (s32[]{:T(128)}, f32[4,64,2,6]{1,2,3,0:T(2,128)S(1)}, f32[4,64,2,6]{1,2,3,0:T(2,128)S(1)}, f32[4,64,2,6,128]{4,3,2,1,0:T(8,128)S(1)}, bf16[64,4,64,2...) while((s32[]{:T(128)}, f32[4,64,2,6]{1,2,3,0:T(2,128)S(1)}, ...), condition=%wide.region_4.5_spmd, body=%wide.region_3.4_spmd.sunk | while | flops 1597445 | bytes 4354199 | solution.py:31
  533.7 2.5 fusion.101
  537.4 2.5 fusion.101
  541.1 2.5 fusion.101
  544.9 2.5 fusion.101
  548.6 2.5 fusion.101
  552.3 2.5 fusion.101
  556.0 2.5 fusion.101
  559.7 2.5 fusion.101
  563.4 2.5 fusion.101
  567.1 2.5 fusion.101
  570.8 2.5 fusion.101
  574.6 2.5 fusion.101
  578.3 2.5 fusion.101
  582.0 2.5 fusion.101
  585.7 2.5 fusion.101
  589.4 2.5 fusion.101
  593.1 2.5 fusion.101
  596.8 2.5 fusion.101
  600.5 2.5 fusion.101
  604.2 2.5 fusion.101
  608.0 2.5 fusion.101
  611.7 2.5 fusion.101
  615.4 2.5 fusion.101
  619.1 2.5 fusion.101
  622.8 2.5 fusion.101
  626.5 2.5 fusion.101
  630.2 2.5 fusion.101
  633.9 2.5 fusion.101
  637.7 2.5 fusion.101
  641.4 2.5 fusion.101
  645.1 2.5 fusion.101
  648.8 2.5 fusion.101
  652.5 2.5 fusion.101
  656.2 2.5 fusion.101
  659.9 2.5 fusion.101
  663.6 2.5 fusion.101
  689.6 2.5 fusion.101
  768.0 3.2 multiply_reduce_fusion.1
  773.7 100.2 %all-gather.9.cloned.1.call-done = bf16[512,1,1536]{2,1,0:T(2,128)(2,1)} async-done(((bf16[4,1,1536]{2,1,0:T(2,128)(2,1)}), bf16[512,1,1536]{2,1,0:T(2,128)(2,1)}) %all-gather.9.cloned.1.call-update) | async-done | bytes 1572880 | tf_op jit(solution)/shard_map/all_gather | solution.py:168
  882.2 3.3 fusion.38
  885.5 150.3 %all-reduce.3.cloned.1.call-done = f32[512,1536]{1,0:T(8,128)} async-done(((f32[512,1536]{1,0:T(8,128)}), f32[512,1536]{1,0:T(8,128)}) %all-reduce.3.cloned.1.call-update) | async-done | bytes 3145744
  (331 shorter events, 169.6 us)
Async XLA Ops:
  6.5 873.4 %copy-start = (bf16[192,1536]{1,0:T(8,128)(2,1)S(1)}, bf16[192,1536]{1,0:T(8,128)(2,1)}, u32[]{:S(2)}) copy-start(bf16[192,1536]{1,0:T(8,128)(2,1)} %param.28) | copy-start | bytes 1769476
  6.5 524.3 %all-gather.7.cloned.1.call-start = ((), (), s32[]{:S(2)}) async-start(), calls=%async_computation | async-start | bytes 68157440 | tf_op jit(solution)/shard_map/all_gather | solution.py:19
  8.2 4.6 copy-start.12
  8.2 6.5 copy-start.1
  12.1 0.6 copy-start.8
  16.7 156.9 %copy-start.2 = (bf16[64,64,256]{2,1,0:T(8,128)(2,1)S(1)}, bf16[64,64,256]{2,1,0:T(8,128)(2,1)}, u32[]{:S(2)}) copy-start(bf16[64,64,256]{2,1,0:T(8,128)(2,1)} %param.19) | copy-start | bytes 6291460
  173.6 2.1 copy-start.7
  175.9 3.4 copy-start.3
  181.4 1.9 copy-start.14
  181.4 2.0 copy-start.11
  181.5 692.5 %all-gather.9.cloned.1.call-start = ((), (), s32[]{:S(2)}) async-start(), calls=%async_computation.1 | async-start | bytes 3170304 | tf_op jit(solution)/shard_map/all_gather | solution.py:168
  333.5 156.5 %copy-start.4 = (bf16[256,64,2,6]{1,2,3,0:T(2,128)(2,1)}, bf16[256,64,2,6]{1,2,3,0:T(2,128)(2,1)S(1)}, u32[]{:S(2)}) copy-start(bf16[256,64,2,6]{1,2,3,0:T(2,128)(2,1)S(1)} %all-gather) | copy-start | bytes 1179652
  489.9 0.9 copy-start.5
  532.5 235.5 %copy-start.9 = (bf16[4,1,1536]{2,0,1:T(4,128)(2,1)S(1)}, bf16[4,1,1536]{2,0,1:T(4,128)(2,1)}, u32[]{:S(2)}) copy-start(bf16[4,1,1536]{2,0,1:T(4,128)(2,1)} %param.16) | copy-start | bytes 36868
  768.0 4.2 copy-start.10
  768.0 105.9 %copy-start.13 = (bf16[1536,32]{0,1:T(8,128)(2,1)S(1)}, bf16[1536,32]{0,1:T(8,128)(2,1)}, u32[]{:S(2)}) copy-start(bf16[1536,32]{0,1:T(8,128)(2,1)} %param.25) | copy-start | bytes 294916
  772.0 263.8 %all-reduce.3.cloned.1.call-start = ((), (), s32[]{:S(2)}) async-start(), calls=%async_computation.2 | async-start | bytes 6291456
  876.4 3.1 copy-start.6
Sparse Core Ops, SparseCore 0:
  181.6 349.2 all-gather.6
  772.1 101.7 all-gather.8
  885.6 150.1 all-reduce.2
where the time goes:
time: 1050 us; the launch traced here: 1040 us
  blocking collectives  461 us (44%)
  waiting for transfers between devices  291 us (28%)
  other arithmetic  218 us (21%)
  local copies, waits for them, and re-layouts  33.8 us (3%)
  matrix products  25 us (2%)
  between operations  13.6 us (1%)
    all_gather x2, blocking collectives, combined_all(): lax.all_gather(a.astype(kind), axis)  305 us
    add x63, other arithmetic, combine_parts(): first[2] * left_scale[..., None] + second[2] * right_scale[..., None]  159 us
    all_gather x1, blocking collectives, on_device(): lax.all_gather(query.reshape(STEPS, rows, QH * HD), 'seq', axis=1, tiled=...  155 us
    unnamed x4, waiting for transfers between devices  150 us
    all_gather x1, waiting for transfers between devices, on_device(): every_row = lax.all_gather(u_tok, ('req', 'seq'), axis=0, tiled=True)  100 us
    add x63, other arithmetic, combine_parts(): first[1] * left_scale + second[1] * right_scale  49.8 us
    all_gather x1, waiting for transfers between devices, combined_all(): lax.all_gather(a.astype(kind), axis)  40 us
  transfers between devices with their start and end apart: 3, of which 3 were waited for; matrix products, arithmetic and copies ran while one was open for 0% of the time, Pallas kernels for 0%

commit v1 on v0

--- a/solution.py
+++ b/solution.py
@@ -12,6 +12,13 @@
 TOP = 4
 STEPS = 4
 MOST = 2
+
+
+def perform_stops_all(page):
+    amount_of = lax.axis_size("seq")
+    xs_all = tuple((amount_of if dd == 1 else 1 for dd in range(page.ndim)))
+    near = jnp.tile(page, xs_all)
+    return lax.all_to_all(near, "seq", split_axis=1, concat_axis=1, tiled=True)
 
 
 def combined_all(value, axis, join):
@@ -111,7 +118,7 @@
         proj[..., QH * HD : (QH + KVH) * HD].reshape(STEPS, rows, KVH, HD), place
     ).astype(jnp.bfloat16)
     fresh_val = proj[..., (QH + KVH) * HD :].reshape(STEPS, rows, KVH, HD).astype(jnp.bfloat16)
-    every_query = lax.all_gather(query.reshape(STEPS, rows, QH * HD), "seq", axis=1, tiled=True)
+    every_query = perform_stops_all(query.reshape(STEPS, rows, QH * HD))
     grouped_all = every_query.reshape(STEPS, group_rows, KVH, heads_per, HD)
     cache_keys = k_cache.reshape(group_rows, local_pos, KVH, HD)
     cache_vals = v_cache.reshape(group_rows, local_pos, KVH, HD)

time: 1050 us -> 894 us (0.85)
  blocking collectives: 461 us -> 307 us
  waiting for transfers between devices: 291 us -> 272 us
  starting transfers between devices: 0.27 us -> 12.3 us
    all_gather x1 -> x0, blocking collectives: 155 us -> none  [on_device(): lax.all_gather(query.reshape(STEPS, rows, QH * HD), 'seq', axis=1, tiled=...]
    all_gather x1, waiting for transfers between devices: 40 us -> 17.2 us  [combined_all(): lax.all_gather(a.astype(kind), axis)]
    all_to_all x0 -> x1, starting transfers between devices: none -> 12 us  [perform_stops_all(): return lax.all_to_all(near, 'seq', split_axis=1, concat_axis=1, tiled=True)]
  transfers between devices with their start and end apart: 3 -> 4, of which waited for: 3 -> 4; matrix products, arithmetic and copies ran while one was open for 0% -> 1% of each run, Pallas kernels for 0% -> 0%
where the time goes in v1:
time: 894 us; the launch traced here: 884 us
  blocking collectives  307 us (34%)
  waiting for transfers between devices  272 us (30%)
  other arithmetic  218 us (24%)
  local copies, waits for them, and re-layouts  35.6 us (4%)
  matrix products  24.2 us (3%)
  between operations  13.6 us (2%)
  starting transfers between devices  12.3 us (1%)
    all_gather x2, blocking collectives, combined_all(): lax.all_gather(a.astype(kind), axis)  307 us
    add x63, other arithmetic, combine_parts(): first[2] * left_scale[..., None] + second[2] * right_scale[..., None]  159 us
    unnamed x4, waiting for transfers between devices  150 us
    all_gather x1, waiting for transfers between devices, on_device(): every_row = lax.all_gather(u_tok, ('req', 'seq'), axis=0, tiled=True)  96.3 us
    add x63, other arithmetic, combine_parts(): first[1] * left_scale + second[1] * right_scale  49.8 us
  transfers between devices with their start and end apart: 4, of which 4 were waited for; matrix products, arithmetic and copies ran while one was open for 1% of the time, Pallas kernels for 0%

profile of v1, /device:TPU:1, one launch (start us, length us, event | category | flops | bytes accessed | tf_op | source)
XLA Modules:
  0.0 884.0 jit_solution(559090187998053290)
XLA Ops:
  8.2 3.8 convolution_bitcast_fusion.1
  14.6 12.0 %all-to-all-start = ((bf16[4,64,1536]{2,0,1:T(4,128)(2,1)}), bf16[4,64,1536]{2,0,1:T(4,128)(2,1)S(1)}, u32[]{:S(2)}, u32[]{:S(2)}) async-start(bf16[4,64,1536]{2,0,1:T(4,128)(2,1)} %tile.2), calls=%async_computation | async-start | bytes 1572864 | tf_op jit(solution)/shard_map/all_to_all | solution.py:21
  29.2 4.0 reshape.422
  33.5 8.0 all-to-all-done
  43.0 3.4 fusion.8
  51.0 151.7 %all-gather = bf16[256,64,2,6]{1,2,3,0:T(2,128)(2,1)S(1)} all-gather(bf16[4,64,2,6]{1,2,3,0:T(2,128)(2,1)S(1)} %copy.157), channel_id=2, replica_groups=mesh['req'=2,'seq'=64] {'seq'}, dimensions={0}, use_global_device_ids=true | all-gather | bytes 399360 | tf_op jit(solution)/shard_map/all_gather | solution.py:26
  202.7 155.0 %all-gather.1 = bf16[256,64,2,6]{1,2,3,0:T(2,128)(2,1)S(1)} all-gather(bf16[4,64,2,6]{1,2,3,0:T(2,128)(2,1)S(1)} %copy.159), channel_id=3, replica_groups=mesh['req'=2,'seq'=64] {'seq'}, dimensions={0}, use_global_device_ids=true | all-gather | bytes 399360 | tf_op jit(solution)/shard_map/all_gather | solution.py:26
  358.6 17.2 %all-gather.7.cloned.1.call-done = bf16[256,64,2,6,128]{4,3,0,2,1:T(8,128)(2,1)} async-done(((bf16[4,64,2,6,128]{4,3,0,2,1:T(8,128)(2,1)}), bf16[256,64,2,6,128]{4,3,0,2,1:T(8,128)(2,1)}) %all-gather.7.cloned.1.call-update) | async-done | bytes 50331664 | tf_op jit(solution)/shard_map/all_gather | solution.py:26
  377.4 233.8 %while.19 = (s32[]{:T(128)}, f32[4,64,2,6]{1,2,3,0:T(2,128)S(1)}, f32[4,64,2,6]{1,2,3,0:T(2,128)S(1)}, f32[4,64,2,6,128]{4,3,2,1,0:T(8,128)S(1)}, bf16[64,4,64,2...) while((s32[]{:T(128)}, f32[4,64,2,6]{1,2,3,0:T(2,128)S(1)}, ...), condition=%wide.region_4.5_spmd, body=%wide.region_3.4_spmd.sunk | while | flops 1597445 | bytes 4354199 | solution.py:38
  378.6 2.5 fusion.101
  382.3 2.5 fusion.101
  386.1 2.5 fusion.101
  389.8 2.5 fusion.101
  393.5 2.5 fusion.101
  397.2 2.5 fusion.101
  400.9 2.5 fusion.101
  404.6 2.5 fusion.101
  408.3 2.5 fusion.101
  412.0 2.5 fusion.101
  415.7 2.5 fusion.101
  419.5 2.5 fusion.101
  423.2 2.5 fusion.101
  426.9 2.5 fusion.101
  430.6 2.5 fusion.101
  434.3 2.5 fusion.101
  438.0 2.5 fusion.101
  441.7 2.5 fusion.101
  445.4 2.5 fusion.101
  449.2 2.5 fusion.101
  452.9 2.5 fusion.101
  456.6 2.5 fusion.101
  460.3 2.5 fusion.101
  464.0 2.5 fusion.101
  467.7 2.5 fusion.101
  471.4 2.5 fusion.101
  475.1 2.5 fusion.101
  478.8 2.5 fusion.101
  482.6 2.5 fusion.101
  486.3 2.5 fusion.101
  490.0 2.5 fusion.101
  493.7 2.5 fusion.101
  497.4 2.5 fusion.101
  501.1 2.5 fusion.101
  541.9 2.5 fusion.101
  612.3 3.2 multiply_reduce_fusion.1
  617.9 96.3 %all-gather.9.cloned.1.call-done = bf16[512,1,1536]{2,1,0:T(2,128)(2,1)} async-done(((bf16[4,1,1536]{2,1,0:T(2,128)(2,1)}), bf16[512,1,1536]{2,1,0:T(2,128)(2,1)}) %all-gather.9.cloned.1.call-update) | async-done | bytes 1572880 | tf_op jit(solution)/shard_map/all_gather | solution.py:175
  722.4 3.3 fusion.38
  725.7 150.3 %all-reduce.3.cloned.1.call-done = f32[512,1536]{1,0:T(8,128)} async-done(((f32[512,1536]{1,0:T(8,128)}), f32[512,1536]{1,0:T(8,128)}) %all-reduce.3.cloned.1.call-update) | async-done | bytes 3145744
  (329 shorter events, 171.7 us)
Async XLA Ops:
  6.5 713.7 %copy-start = (bf16[192,1536]{1,0:T(8,128)(2,1)S(1)}, bf16[192,1536]{1,0:T(8,128)(2,1)}, u32[]{:S(2)}) copy-start(bf16[192,1536]{1,0:T(8,128)(2,1)} %param.28) | copy-start | bytes 1769476
  8.1 3.8 copy-start.9
  11.9 15.2 %copy-start.1 = (bf16[64,64,256]{2,1,0:T(8,128)(2,1)S(1)}, bf16[64,64,256]{2,1,0:T(8,128)(2,1)}, u32[]{:S(2)}) copy-start(bf16[64,64,256]{2,1,0:T(8,128)(2,1)} %param.18) | copy-start | bytes 6291460
  14.6 26.9 %all-to-all-start = ((bf16[4,64,1536]{2,0,1:T(4,128)(2,1)}), bf16[4,64,1536]{2,0,1:T(4,128)(2,1)S(1)}, u32[]{:S(2)}, u32[]{:S(2)}) async-start(bf16[4,64,1536]{2,0,1:T(4,128)(2,1)} %tile.2), calls=%async_computation | async-start | bytes 1572864 | tf_op jit(solution)/shard_map/all_to_all | solution.py:21
  26.6 349.2 %all-gather.7.cloned.1.call-start = ((), (), s32[]{:S(2)}) async-start(), calls=%async_computation.1 | async-start | bytes 68157440 | tf_op jit(solution)/shard_map/all_gather | solution.py:26
  29.2 4.1 copy-start.10
  43.0 3.4 copy-start.2
  46.4 2.2 copy-start.12
  46.5 2.3 copy-start.8
  48.6 665.6 %all-gather.9.cloned.1.call-start = ((), (), s32[]{:S(2)}) async-start(), calls=%async_computation.2 | async-start | bytes 3170304 | tf_op jit(solution)/shard_map/all_gather | solution.py:175
  202.7 155.0 %copy-start.3 = (bf16[256,64,2,6]{1,2,3,0:T(2,128)(2,1)}, bf16[256,64,2,6]{1,2,3,0:T(2,128)(2,1)S(1)}, u32[]{:S(2)}) copy-start(bf16[256,64,2,6]{1,2,3,0:T(2,128)(2,1)S(1)} %all-gather) | copy-start | bytes 1179652
  357.7 0.9 copy-start.4
  377.4 234.8 %copy-start.6 = (bf16[4,1,1536]{2,0,1:T(4,128)(2,1)S(1)}, bf16[4,1,1536]{2,0,1:T(4,128)(2,1)}, u32[]{:S(2)}) copy-start(bf16[4,1,1536]{2,0,1:T(4,128)(2,1)} %param.16) | copy-start | bytes 36868
  612.2 4.2 copy-start.7
  612.3 102.0 %copy-start.11 = (bf16[1536,32]{0,1:T(8,128)(2,1)S(1)}, bf16[1536,32]{0,1:T(8,128)(2,1)}, u32[]{:S(2)}) copy-start(bf16[1536,32]{0,1:T(8,128)(2,1)} %param.25) | copy-start | bytes 294916
  616.2 259.8 %all-reduce.3.cloned.1.call-start = ((), (), s32[]{:S(2)}) async-start(), calls=%async_computation.3 | async-start | bytes 6291456
  716.7 3.1 copy-start.5
Sparse Core Ops, SparseCore 0:
  48.7 327.0 all-gather.6
  616.3 97.8 all-gather.8
  725.9 150.1 all-reduce.2
